TPU v7x, 128 devices: a whole 4x4x4 slice. The times are simulated.
128 devices in a mesh: sta: 2 (over x_lo), gx: 16 (over x_hi, z, core), gy: 4 (over y).
Axes of the slice: x: 4 (x_hi: 2, x_lo: 2; x = x_hi * 2 + x_lo), y: 4, z: 4, core: 2. Of those that a mesh axis runs over, the one named last changes fastest.
Arguments:
- record: float32 [128, 1024], replicated, may hold values from -6 to 6
- shifts: int32 [128, 256], P(None, 'gx'), may hold values from 0 to 1022
- station_group: int32 [128], replicated, may hold values from 0 to 7
- weights: bfloat16 [128, 256, 512], P('sta', 'gy'), may hold values from -6 to 6
- psf_real: float32 [256, 256, 512], P(None, 'gx', 'gy'), may hold values from -6 to 6
- psf_imag: float32 [256, 256, 512], P(None, 'gx', 'gy'), may hold values from -6 to 6
Outputs:
- image: float32 [2, 256, 256, 512], P('sta', 'gx', 'gy')
All inputs are finite; a program needn't handle non-finite values.
Results may differ from a plain program's by a relative error of at most 0.0029.
Values may be sent and summed in bfloat16 or wider, within the bound.
No kernel may reach another device: no remote copies, remote signals or barrier semaphores. Data moves between devices by JAX's collectives and lax.ppermute only.
A program may use at most 128 MiB of HBM per device.

v0:
```python
import math
import jax
import jax.numpy as jnp
from jax import lax
from jax.sharding import PartitionSpec as P

T_DEV = 1
NZ = 256
NX = 256
GROUPS = 8
NOISE_POWER = 0.25
HIGHEST = lax.Precision.HIGHEST


def station_counts(station_group):
    labels = jnp.arange(GROUPS, dtype=jnp.int32)
    onehot = (station_group[:, None] == labels[None, :]).astype(jnp.float32)
    totals = jnp.sum(onehot, axis=0)
    return jnp.dot(onehot, totals, precision=HIGHEST)


def coefficients(record, shifts, per_station, first_time, num_times):
    times_range = first_time + jnp.arange(num_times, dtype=jnp.int32)
    positions = shifts[:, :, None] + times_range[None, None, :]
    values = jnp.take_along_axis(record, positions.reshape(positions.shape[0], -1), axis=1)
    scaled = values.reshape(positions.shape) / per_station[:, None, None]
    return jnp.transpose(scaled, (2, 1, 0)).astype(jnp.bfloat16)


def fourier_parts(length, scale):
    indices = jnp.arange(length, dtype=jnp.int32)
    product = indices[:, None] * indices[None, :] % length
    angles = product.astype(jnp.float32) * (2.0 * math.pi / length)
    return (jnp.cos(angles) * scale, jnp.sin(angles) * scale)


def complex_table(length, forward):
    if forward:
        cosine, sine = fourier_parts(length, 1.0)
        return jnp.stack([jnp.stack([cosine, sine]), jnp.stack([-sine, cosine])])
    cosine, sine = fourier_parts(length, 1.0 / length)
    return jnp.stack([jnp.stack([cosine, -sine]), jnp.stack([sine, cosine])])


def along_rows(piece, table):
    return jnp.einsum("itzny,oikn->otzky", piece, table, precision=HIGHEST)


def along_depth(piece, table):
    return jnp.einsum("itnxy,oikn->otkxy", piece, table, precision=HIGHEST)


def on_device(record, shifts, station_group, weights, psf_real, psf_imag):
    per_station = station_counts(station_group)
    depth_rows = shifts.shape[1]
    lateral_rows = weights.shape[1]
    width_y = weights.shape[2]
    columns = lateral_rows * width_y
    first_time = lax.axis_index("sta") * T_DEV
    coefficient = coefficients(record, shifts, per_station, first_time, T_DEV)
    coefficient = coefficient.reshape(T_DEV * depth_rows, coefficient.shape[2])
    piece = lax.all_gather(weights, "sta", axis=0, tiled=True)
    stack = jnp.dot(
        coefficient, piece.reshape(piece.shape[0], columns), preferred_element_type=jnp.float32
    )
    stack = stack.reshape(T_DEV, depth_rows, lateral_rows, width_y)
    cosine_y, sine_y = fourier_parts(width_y, 1.0)
    spectrum = jnp.einsum(
        "tzxn,okn->otzxk", stack, jnp.stack([cosine_y, -sine_y]), precision=HIGHEST
    )
    row_table = complex_table(NX, True)
    by_rows = along_rows(
        lax.all_to_all(spectrum, "gy", split_axis=4, concat_axis=3, tiled=True), row_table
    )
    depth_table = complex_table(NZ, True)
    by_depth = along_depth(
        lax.all_to_all(by_rows, "gx", split_axis=3, concat_axis=2, tiled=True), depth_table
    )
    power = psf_real * psf_real + psf_imag * psf_imag + NOISE_POWER
    filt_real = (psf_real * by_depth[0] + psf_imag * by_depth[1]) / power
    filt_imag = (psf_real * by_depth[1] - psf_imag * by_depth[0]) / power
    back_depth = along_depth(jnp.stack([filt_real, filt_imag]), complex_table(NZ, False))
    back_table = complex_table(NX, False)
    back_rows = along_rows(
        lax.all_to_all(back_depth, "gx", split_axis=2, concat_axis=3, tiled=True), back_table
    )
    cosine_back, sine_back = fourier_parts(width_y, 1.0 / width_y)
    real_table = jnp.stack([cosine_back, -sine_back])
    return jnp.einsum(
        "itzxk,iyk->tzxy",
        lax.all_to_all(back_rows, "gy", split_axis=3, concat_axis=4, tiled=True),
        real_table,
        precision=HIGHEST,
    )


def solution(mesh):
    in_specs = (
        P(),
        P(None, "gx"),
        P(),
        P("sta", "gy", None),
        P(None, "gx", "gy"),
        P(None, "gx", "gy"),
    )
    out_specs = P("sta", "gx", "gy", None)
    return jax.shard_map(
        on_device, mesh=mesh, in_specs=in_specs, out_specs=out_specs, check_vma=False
    )
```

profile of v0, /device:TPU:0, one launch (start us, length us, event | category | flops | bytes accessed | tf_op | source)
XLA Modules:
  0.0 516.7 jit_solution(10342550417236700609)
XLA Ops:
  7.6 16.6 %gather_fusion = f32[2048]{0:T(1024)S(1)} fusion(f32[128,1024]{1,0:T(8,128)S(1)} %copy-done, s32[2048]{0:T(1024)S(1)} %reshape.275), kind=kCustom, calls=%fused_computation | custom fusion | bytes 32768 | tf_op jit(solution)/shard_map/jit(take_along_axis)/gather | solution.py:25
  24.6 4.1 fusion.27
  28.7 89.3 %all-gather.2.cloned.1.call-done = bf16[128,64,512]{2,1,0:T(8,128)(2,1)} async-done(((bf16[64,64,512]{2,1,0:T(8,128)(2,1)}), bf16[128,64,512]{2,1,0:T(8,128)(2,1)}) %all-gather.2.cloned.1.call-update) | async-done | bytes 8388624 | tf_op jit(solution)/shard_map/all_gather | solution.py:62
  118.0 13.1 %copy.78 = bf16[128,64,512]{0,2,1:T(8,128)(2,1)} copy(bf16[128,64,512]{2,1,0:T(8,128)(2,1)} %all-gather.2.cloned.1.call-done) | data formatting | bytes 16777216 | tf_op jit(solution)/shard_map/reshape | solution.py:64
  131.1 5.8 %fusion = f32[16,64,512]{2,0,1:T(8,128)S(1)} fusion(bf16[128,64,512]{0,2,1:T(8,128)(2,1)} %copy.78, f32[128,16]{1,0:T(8,128)S(1)} %reshape.278, s32[128,16]{1,0:T(8,128)S(1)} %copy.50, f32[128]{0:T(128)S(1)} %convolution_bitcast_fusion.4, s32[]{:T(128)S(6)} %axis_index.15), kind=kOutput, calls=%fused_computation.1 | convolution fusion | flops 134238208 | bytes 10502660 | tf_op jit(solution)/shard_map/dot_general | solution.py:63
  136.9 9.2 %convolution_bitcast_fusion = f32[2,1,16,64,512]{4,3,2,0,1:T(8,128)} fusion(f32[1,512,512]{2,1,0:T(8,128)S(1)} %get-tuple-element.12, f32[1,512,512]{2,1,0:T(8,128)S(1)} %get-tuple-element.11, f32[16,64,512]{2,0,1:T(8,128)S(1)} %fusion), kind=kOutput, calls=%fused_computation.8 | convolution fusion | flops 6442975232 | bytes 8388608 | tf_op jit(solution)/shard_map/tzxn,okn->otzxk/dot_general | solution.py:68
  146.0 9.1 %copy.54 = f32[2,1,16,64,512]{3,2,0,1,4:T(8,128)} copy(f32[2,1,16,64,512]{4,3,2,0,1:T(8,128)} %convolution_bitcast_fusion) | data formatting | bytes 8388608 | tf_op jit(solution)/shard_map/tzxn,okn->otzxk/transpose | solution.py:68
  155.2 19.9 %reshape.303 = f32[4,1,262144]{2,1,0:T(1,128)} reshape(f32[512,1,2,16,64]{4,3,2,1,0:T(8,128)} %bitcast.153) | data formatting | bytes 8388608
  175.1 4.8 all-to-all-start
  182.1 47.0 %all-to-all-done = f32[4,1,262144]{2,1,0:T(1,128)} async-done(((f32[4,1,262144]{2,1,0:T(1,128)}), f32[4,1,262144]{2,1,0:T(1,128)}, u32[]{:S(2)}, u32[]{:S(2)}) %all-to-all-start) | async-done | bytes 4194336 | tf_op jit(solution)/shard_map/all_to_all | solution.py:73
  229.6 15.2 %reduce = f32[4,262144]{1,0:T(4,128)} reduce(f32[4,1,262144]{2,1,0:T(1,128)} %all-to-all-done, f32[]{:T(128)} %broadcast.479), dimensions={1}, to_apply=%all_to_all.44.reduce_sub_computation | reduce | bytes 8388612 | tf_op jit(solution)/shard_map/all_to_all | solution.py:73
  244.8 9.3 %reshape.304 = f32[512,1,2,16,64]{4,3,2,1,0:T(8,128)} reshape(f32[4,262144]{1,0:T(4,128)} %reduce) | data formatting | bytes 8388608
  254.1 6.9 %copy.55 = f32[2,1,16,64,4,128]{5,3,4,0,2,1:T(8,128)} copy(f32[2,1,16,64,4,128]{3,2,0,5,4,1:T(8,128)} %bitcast.154) | data formatting | bytes 8388608 | tf_op jit(solution)/shard_map/all_to_all | solution.py:73
  261.0 8.7 %convolution_bitcast_fusion.3 = f32[2,1,16,256,128]{4,3,2,0,1:T(8,128)S(1)} fusion(f32[2,16,256,128,1]{3,2,0,1,4:T(8,128)} %bitcast.155, f32[1,2,256,256]{3,2,1,0:T(8,128)S(1)} %get-tuple-element.10, f32[1,2,256,256]{3,2,1,0:T(8,128)S(1)} %get-tuple-element.9), kind=kOutput, calls=%fused_computation.12 | convolution fusion | flops 6442713088 | bytes 9437184 | tf_op jit(solution)/shard_map/itzny,oikn->otzky/dot_general | solution.py:46
  269.7 4.4 copy.56
  274.1 6.9 %all-to-all-start.1 = ((f32[2,1,16,256,128]{4,2,0,1,3:T(8,128)}), f32[2,1,16,256,128]{4,2,0,1,3:T(8,128)}, u32[]{:S(2)}, u32[]{:S(2)}) async-start(f32[2,1,16,256,128]{4,2,0,1,3:T(8,128)} %copy.56), calls=%async_computation.1 | async-start | bytes 8388608 | tf_op jit(solution)/shard_map/all_to_all | solution.py:77
  282.0 1.1 broadcast_multiply_fusion.1
  283.1 53.2 %all-to-all-done.1 = f32[2,1,16,256,128]{4,2,0,1,3:T(8,128)} async-done(((f32[2,1,16,256,128]{4,2,0,1,3:T(8,128)}), f32[2,1,16,256,128]{4,2,0,1,3:T(8,128)}, u32[]{:S(2)}, u32[]{:S(2)}) %all-to-all-start.1) | async-done | bytes 4194336 | tf_op jit(solution)/shard_map/all_to_all | solution.py:77
  336.3 2.7 copy.57
  339.1 7.1 %convolution_bitcast_fusion.2 = f32[2,256,16,128]{3,1,2,0:T(8,128)S(1)} fusion(f32[2,256,16,128,1]{3,1,0,2,4:T(8,128)S(1)} %bitcast.157, f32[1,2,256,256]{3,2,1,0:T(8,128)S(1)} %get-tuple-element.10, f32[1,2,256,256]{3,2,1,0:T(8,128)S(1)} %get-tuple-element.9), kind=kOutput, calls=%fused_computation.11 | convolution fusion | flops 6442713088 | bytes 9437184 | tf_op jit(solution)/shard_map/itnxy,oikn->otkxy/dot_general | solution.py:50
  346.2 1.5 fusion.13
  347.7 7.3 %fusion.5 = f32[2,1,256,16,128]{4,2,3,0,1:T(8,128)S(1)} fusion(f32[1,2,256,256]{3,2,1,0:T(8,128)S(1)} %get-tuple-element.8, f32[1,2,256,256]{3,2,1,0:T(8,128)S(1)} %get-tuple-element.7, f32[1,1,256,16,128]{4,2,3,1,0:T(8,128)S(1)} %get-tuple-element.6, f32[1,1,256,16,128]{4,2,3,1,0:T(8,128)S(1)} %get-tuple-element.5), kind=kOutput, calls=%fused_computation.9 | convolution fusion | flops 6443761664 | bytes 9437184 | tf_op jit(solution)/shard_map/itnxy,oikn->otkxy/dot_general | solution.py:50
  355.0 2.4 copy.64
  357.5 64.3 %all_to_all.60 = f32[2,1,256,16,128]{4,3,0,1,2:T(8,128)S(1)} all-to-all(f32[2,1,256,16,128]{4,3,0,1,2:T(8,128)S(1)} %copy.64), channel_id=1, replica_groups=mesh['sta'=2,'gx'=16,'gy'=4] {'gx'}, dimensions={2} | all-to-all | bytes 8388608 | tf_op jit(solution)/shard_map/all_to_all | solution.py:85
  422.3 6.9 %convolution_bitcast_fusion.1 = f32[2,1,16,256,128]{4,3,2,0,1:T(8,128)S(1)} fusion(f32[2,16,256,128,1]{3,2,0,1,4:T(8,128)S(1)} %bitcast.156, f32[1,2,256,256]{3,2,1,0:T(8,128)S(1)} %get-tuple-element.8, f32[1,2,256,256]{3,2,1,0:T(8,128)S(1)} %get-tuple-element.7), kind=kOutput, calls=%fused_computation.10 | convolution fusion | flops 6442713088 | bytes 9437184 | tf_op jit(solution)/shard_map/itzny,oikn->otzky/dot_general | solution.py:46
  429.2 4.4 copy.66
  433.6 5.1 all-to-all-start.3
  438.7 4.2 multiply_negate_fusion
  442.8 44.5 %all-to-all-done.3 = f32[2,1,16,256,128]{4,2,0,1,3:T(8,128)} async-done(((f32[2,1,16,256,128]{4,2,0,1,3:T(8,128)}), f32[2,1,16,256,128]{4,2,0,1,3:T(8,128)}, u32[]{:S(2)}, u32[]{:S(2)}) %all-to-all-start.3) | async-done | bytes 4194336 | tf_op jit(solution)/shard_map/all_to_all | solution.py:91
  487.3 6.9 %copy.94 = f32[2,1,16,4,64,128]{5,3,4,0,2,1:T(4,128)} copy(f32[2,1,16,4,64,128]{5,2,0,4,3,1:T(8,128)} %bitcast.57) | data formatting | bytes 8388608 | tf_op jit(solution)/shard_map/all_to_all | solution.py:91
  494.2 5.5 %reshape.274 = f32[2,16,64,512]{3,2,0,1:T(8,128)} reshape(f32[2,1,16,64,4,128]{5,4,3,0,2,1:T(4,128)} %bitcast.159) | data formatting | bytes 8388608 | tf_op jit(solution)/shard_map/reshape.27
  499.7 9.9 %fusion.19 = f32[1,16,64,512]{3,2,1,0:T(8,128)} fusion(f32[2,16,64,512]{3,2,0,1:T(8,128)} %reshape.274, f32[1,512,512]{2,1,0:T(8,128)S(1)} %get-tuple-element.17, f32[1,512,512]{2,1,0:T(8,128)S(1)} %get-tuple-element.18), kind=kOutput, calls=%fused_computation.33 | convolution fusion | flops 6442975232 | bytes 8388608 | tf_op jit(solution)/shard_map/itzxk,iyk->tzxy/dot_general | solution.py:89
  (27 shorter events, 5.6 us)
Async XLA Ops:
  6.5 1.1 copy-start
  6.5 0.8 copy-start.4
  6.5 111.5 %all-gather.2.cloned.1.call-start = ((), (), s32[]{:S(2)}) async-start(), calls=%async_computation.4 | async-start | bytes 12582912 | tf_op jit(solution)/shard_map/all_gather | solution.py:62
  7.6 16.7 %copy-start.5 = (s32[128]{0:T(128)S(1)}, s32[128]{0:T(128)}, u32[]{:S(2)}) copy-start(s32[128]{0:T(128)} %param.8) | copy-start | bytes 1540
  175.1 54.0 %all-to-all-start = ((f32[4,1,262144]{2,1,0:T(1,128)}), f32[4,1,262144]{2,1,0:T(1,128)}, u32[]{:S(2)}, u32[]{:S(2)}) async-start(f32[4,1,262144]{2,1,0:T(1,128)} %reshape.303), calls=%async_computation | async-start | bytes 8388608 | tf_op jit(solution)/shard_map/all_to_all | solution.py:73
  274.1 62.2 %all-to-all-start.1 = ((f32[2,1,16,256,128]{4,2,0,1,3:T(8,128)}), f32[2,1,16,256,128]{4,2,0,1,3:T(8,128)}, u32[]{:S(2)}, u32[]{:S(2)}) async-start(f32[2,1,16,256,128]{4,2,0,1,3:T(8,128)} %copy.56), calls=%async_computation.1 | async-start | bytes 8388608 | tf_op jit(solution)/shard_map/all_to_all | solution.py:77
  339.0 7.2 %copy-start.2 = (f32[256,16,128]{2,1,0:T(8,128)S(1)}, f32[256,16,128]{2,1,0:T(8,128)}, u32[]{:S(2)}) copy-start(f32[256,16,128]{2,1,0:T(8,128)} %param.11) | copy-start | bytes 6291460
  339.0 7.2 %copy-start.3 = (f32[256,16,128]{2,1,0:T(8,128)S(1)}, f32[256,16,128]{2,1,0:T(8,128)}, u32[]{:S(2)}) copy-start(f32[256,16,128]{2,1,0:T(8,128)} %param.10) | copy-start | bytes 6291460
  433.6 53.7 %all-to-all-start.3 = ((f32[2,1,16,256,128]{4,2,0,1,3:T(8,128)}), f32[2,1,16,256,128]{4,2,0,1,3:T(8,128)}, u32[]{:S(2)}, u32[]{:S(2)}) async-start(f32[2,1,16,256,128]{4,2,0,1,3:T(8,128)} %copy.66), calls=%async_computation.3 | async-start | bytes 8388608 | tf_op jit(solution)/shard_map/all_to_all | solution.py:91
  499.7 9.9 %copy-start.1 = (f32[128,1024]{1,0:T(8,128)S(1)}, f32[128,1024]{1,0:T(8,128)}, u32[]{:S(2)}) copy-start(f32[128,1024]{1,0:T(8,128)} %param.6) | copy-start | bytes 1572868
Sparse Core Ops, SparseCore 0:
  9.0 108.9 all-gather.1
where the time goes:
time: 526 us; the launch traced here: 517 us
  waiting for transfers between devices  235 us (45%)
  local copies, waits for them, and re-layouts  103 us (20%)
  blocking collectives  64.3 us (12%)
  matrix products  55 us (10%)
  other arithmetic  29.4 us (6%)
  starting transfers between devices  16.8 us (3%)
  between operations  13.8 us (3%)
    all_gather x1, waiting for transfers between devices, on_device(): piece = lax.all_gather(weights, 'sta', axis=0, tiled=True)  89.3 us
    all_to_all x1, blocking collectives, on_device(): lax.all_to_all(back_depth, 'gx', split_axis=2, concat_axis=3, tiled=True)  64.3 us
    all_to_all x1, waiting for transfers between devices, on_device(): lax.all_to_all(by_rows, 'gx', split_axis=3, concat_axis=2, tiled=True)  53.2 us
    all_to_all x1, waiting for transfers between devices, on_device(): lax.all_to_all(spectrum, 'gy', split_axis=4, concat_axis=3, tiled=True)  47 us
    all_to_all x1, waiting for transfers between devices, on_device(): lax.all_to_all(back_rows, 'gy', split_axis=3, concat_axis=4, tiled=True)  44.5 us
    unnamed x15, local copies, waits for them, and re-layouts  29.4 us
    gather x3, local copies, waits for them, and re-layouts, coefficients(): jnp.take_along_axis(record, positions.reshape(positions.shape[0], -1), ax...  16.8 us
    dot_general x2, matrix products, along_rows(): return jnp.einsum('itzny,oikn->otzky', piece, table, precision=HIGHEST)  15.6 us
  transfers between devices with their start and end apart: 4, of which 4 were waited for; matrix products, arithmetic and copies ran while one was open for 6% of the time, Pallas kernels for 0%

commit v1 on v0

--- a/solution.py
+++ b/solution.py
@@ -59,7 +59,9 @@
     first_time = lax.axis_index("sta") * T_DEV
     coefficient = coefficients(record, shifts, per_station, first_time, T_DEV)
     coefficient = coefficient.reshape(T_DEV * depth_rows, coefficient.shape[2])
-    piece = lax.all_gather(weights, "sta", axis=0, tiled=True)
+    piece = jnp.concatenate(
+        lax.all_to_all(jnp.stack([weights] * lax.axis_size("sta")), "sta", 0, 0), axis=0
+    )
     stack = jnp.dot(
         coefficient, piece.reshape(piece.shape[0], columns), preferred_element_type=jnp.float32
     )

time: 526 us -> 510 us (0.970)
  waiting for transfers between devices: 235 us -> 215 us
  between operations: 13.8 us -> 0.47 us
  starting transfers between devices: 16.8 us -> 25.4 us
  other arithmetic: 29.4 us -> 36.9 us
    all_gather x1 -> x0, waiting for transfers between devices: 89.3 us -> none  [on_device(): piece = lax.all_gather(weights, 'sta', axis=0, tiled=True)]
    all_to_all x0 -> x1, waiting for transfers between devices: none -> 71.1 us  [on_device(): lax.all_to_all(jnp.stack([weights] * lax.axis_size('sta')), 'sta', 0, 0)]
    reshape x1 -> x0, local copies, waits for them, and re-layouts: 13.1 us -> none  [on_device(): piece.reshape(piece.shape[0], columns)]
    another operation x1 -> x2, local copies, waits for them, and re-layouts: 5.49 us -> 17.9 us  [the longest x1 12.4 us: on_device(): piece.reshape(piece.shape[0], columns)]
    another operation x0 -> x1, other arithmetic: none -> 7.51 us  [on_device(): jnp.stack([weights] * lax.axis_size('sta'))]
    all_to_all x0 -> x1, starting transfers between devices: none -> 7.08 us  [on_device(): lax.all_to_all(jnp.stack([weights] * lax.axis_size('sta')), 'sta', 0, 0)]
    unnamed x15 -> x16, local copies, waits for them, and re-layouts: 29.4 us -> 30.5 us
where the time goes in v1:
time: 510 us; the launch traced here: 500 us
  waiting for transfers between devices  215 us (42%)
  local copies, waits for them, and re-layouts  103 us (20%)
  blocking collectives  64.3 us (13%)
  matrix products  55.3 us (11%)
  other arithmetic  36.9 us (7%)
  starting transfers between devices  25.4 us (5%)
    all_to_all x1, waiting for transfers between devices, on_device(): lax.all_to_all(jnp.stack([weights] * lax.axis_size('sta')), 'sta', 0, 0)  71.1 us
    all_to_all x1, blocking collectives, on_device(): lax.all_to_all(back_depth, 'gx', split_axis=2, concat_axis=3, tiled=True)  64.3 us
    all_to_all x1, waiting for transfers between devices, on_device(): lax.all_to_all(by_rows, 'gx', split_axis=3, concat_axis=2, tiled=True)  53.1 us
    all_to_all x1, waiting for transfers between devices, on_device(): lax.all_to_all(spectrum, 'gy', split_axis=4, concat_axis=3, tiled=True)  46.3 us
    all_to_all x1, waiting for transfers between devices, on_device(): lax.all_to_all(back_rows, 'gy', split_axis=3, concat_axis=4, tiled=True)  44.5 us
    unnamed x16, local copies, waits for them, and re-layouts  30.5 us
    gather x3, local copies, waits for them, and re-layouts, coefficients(): jnp.take_along_axis(record, positions.reshape(positions.shape[0], -1), ax...  16.8 us
    dot_general x2, matrix products, along_rows(): return jnp.einsum('itzny,oikn->otzky', piece, table, precision=HIGHEST)  15.8 us
  transfers between devices with their start and end apart: 4, of which 4 were waited for; matrix products, arithmetic and copies ran while one was open for 6% of the time, Pallas kernels for 0%

profile of v1, /device:TPU:0, one launch (start us, length us, event | category | flops | bytes accessed | tf_op | source)
XLA Modules:
  0.0 500.3 jit_solution(15269633654173231328)
XLA Ops:
  0.0 7.5 %pad_maximum_fusion = bf16[2,64,64,512]{3,2,1,0:T(8,128)(2,1)} fusion(bf16[1,64,64,512]{3,2,1,0:T(8,128)(2,1)} %bitcast.163), kind=kLoop, calls=%fused_computation.1 | loop fusion | flops 4194304 | bytes 12582912 | tf_op jit(solution)/shard_map/stack | solution.py:63
  7.5 7.1 %all-to-all-start = ((bf16[2,64,64,512]{3,2,1,0:T(8,128)(2,1)}), bf16[2,64,64,512]{3,2,1,0:T(8,128)(2,1)}, u32[]{:S(2)}, u32[]{:S(2)}) async-start(bf16[2,64,64,512]{3,2,1,0:T(8,128)(2,1)} %pad_maximum_fusion), calls=%async_computation | async-start | bytes 16777216 | tf_op jit(solution)/shard_map/all_to_all | solution.py:63
  14.9 16.6 %gather_fusion = f32[2048]{0:T(1024)S(1)} fusion(f32[128,1024]{1,0:T(8,128)S(1)} %copy-done, s32[2048]{0:T(1024)S(1)} %reshape.271), kind=kCustom, calls=%fused_computation | custom fusion | bytes 32768 | tf_op jit(solution)/shard_map/jit(take_along_axis)/gather | solution.py:25
  31.8 4.1 fusion.25
  36.0 71.1 %all-to-all-done = bf16[2,64,64,512]{3,2,1,0:T(8,128)(2,1)} async-done(((bf16[2,64,64,512]{3,2,1,0:T(8,128)(2,1)}), bf16[2,64,64,512]{3,2,1,0:T(8,128)(2,1)}, u32[]{:S(2)}, u32[]{:S(2)}) %all-to-all-start) | async-done | bytes 8388640 | tf_op jit(solution)/shard_map/all_to_all | solution.py:63
  107.1 12.5 %copy.78 = bf16[16,8,64,512]{3,1,2,0:T(8,128)(2,1)} copy(bf16[16,8,64,512]{3,2,1,0:T(8,128)(2,1)} %bitcast.79) | data formatting | bytes 16777216
  119.5 12.4 %copy.51 = bf16[128,32768]{0,1:T(8,128)(2,1)} copy(bf16[128,32768]{1,0:T(8,128)(2,1)} %bitcast.157) | data formatting | bytes 16777216 | tf_op jit(solution)/shard_map/reshape;reshape | solution.py:66
  131.9 5.8 %fusion.37 = f32[16,64,512]{2,0,1:T(8,128)S(1)} fusion(bf16[64,512,128]{2,1,0:T(8,128)(2,1)} %bitcast.156, f32[128,16]{1,0:T(8,128)S(1)} %reshape.274, s32[128,16]{1,0:T(8,128)S(1)} %copy.50, f32[128]{0:T(128)S(1)} %convolution_bitcast_fusion.4, s32[]{:T(128)S(6)} %axis_index.15), kind=kOutput, calls=%fused_computation.72 | convolution fusion | flops 134238208 | bytes 10502660 | tf_op jit(solution)/shard_map/dot_general | solution.py:65
  137.7 9.1 %convolution_bitcast_fusion = f32[2,1,16,64,512]{4,3,2,0,1:T(8,128)} fusion(f32[1,512,512]{2,1,0:T(8,128)S(1)} %get-tuple-element.12, f32[1,512,512]{2,1,0:T(8,128)S(1)} %get-tuple-element.11, f32[16,64,512]{2,0,1:T(8,128)S(1)} %fusion.37), kind=kOutput, calls=%fused_computation.7 | convolution fusion | flops 6442975232 | bytes 8388608 | tf_op jit(solution)/shard_map/tzxn,okn->otzxk/dot_general | solution.py:70
  146.8 9.1 %copy.54 = f32[2,1,16,64,512]{3,2,0,1,4:T(8,128)} copy(f32[2,1,16,64,512]{4,3,2,0,1:T(8,128)} %convolution_bitcast_fusion) | data formatting | bytes 8388608 | tf_op jit(solution)/shard_map/tzxn,okn->otzxk/transpose | solution.py:70
  155.9 8.6 %reshape.299 = f32[4,1,262144]{2,1,0:T(1,128)} reshape(f32[512,1,2,16,64]{4,3,2,1,0:T(8,128)} %bitcast.154) | data formatting | bytes 8388608
  164.6 5.0 %all-to-all-start.1 = ((f32[4,1,262144]{2,1,0:T(1,128)}), f32[4,1,262144]{2,1,0:T(1,128)}, u32[]{:S(2)}, u32[]{:S(2)}) async-start(f32[4,1,262144]{2,1,0:T(1,128)} %reshape.299), calls=%async_computation.1 | async-start | bytes 8388608 | tf_op jit(solution)/shard_map/all_to_all | solution.py:75
  171.7 46.3 %all-to-all-done.1 = f32[4,1,262144]{2,1,0:T(1,128)} async-done(((f32[4,1,262144]{2,1,0:T(1,128)}), f32[4,1,262144]{2,1,0:T(1,128)}, u32[]{:S(2)}, u32[]{:S(2)}) %all-to-all-start.1) | async-done | bytes 4194336 | tf_op jit(solution)/shard_map/all_to_all | solution.py:75
  218.6 15.2 %reduce = f32[4,262144]{1,0:T(4,128)} reduce(f32[4,1,262144]{2,1,0:T(1,128)} %all-to-all-done.1, f32[]{:T(128)} %broadcast.479), dimensions={1}, to_apply=%all_to_all.48.reduce_sub_computation | reduce | bytes 8388612 | tf_op jit(solution)/shard_map/all_to_all | solution.py:75
  233.8 9.3 %reshape.300 = f32[512,1,2,16,64]{4,3,2,1,0:T(8,128)} reshape(f32[4,262144]{1,0:T(4,128)} %reduce) | data formatting | bytes 8388608
  243.0 6.8 %copy.55 = f32[2,1,16,64,4,128]{5,3,4,0,2,1:T(8,128)} copy(f32[2,1,16,64,4,128]{3,2,0,5,4,1:T(8,128)} %bitcast.155) | data formatting | bytes 8388608 | tf_op jit(solution)/shard_map/all_to_all | solution.py:75
  249.9 8.9 %convolution_bitcast_fusion.3 = f32[2,1,16,256,128]{4,3,2,0,1:T(8,128)S(1)} fusion(f32[2,16,256,128,1]{3,2,0,1,4:T(8,128)} %bitcast.158, f32[1,2,256,256]{3,2,1,0:T(8,128)S(1)} %get-tuple-element.10, f32[1,2,256,256]{3,2,1,0:T(8,128)S(1)} %get-tuple-element.9), kind=kOutput, calls=%fused_computation.11 | convolution fusion | flops 6442713088 | bytes 9437184 | tf_op jit(solution)/shard_map/itzny,oikn->otzky/dot_general | solution.py:46
  258.8 4.4 copy.56
  263.2 8.2 %all-to-all-start.2 = ((f32[2,1,16,256,128]{4,2,0,1,3:T(8,128)}), f32[2,1,16,256,128]{4,2,0,1,3:T(8,128)}, u32[]{:S(2)}, u32[]{:S(2)}) async-start(f32[2,1,16,256,128]{4,2,0,1,3:T(8,128)} %copy.56), calls=%async_computation.2 | async-start | bytes 8388608 | tf_op jit(solution)/shard_map/all_to_all | solution.py:79
  273.6 53.1 %all-to-all-done.2 = f32[2,1,16,256,128]{4,2,0,1,3:T(8,128)} async-done(((f32[2,1,16,256,128]{4,2,0,1,3:T(8,128)}), f32[2,1,16,256,128]{4,2,0,1,3:T(8,128)}, u32[]{:S(2)}, u32[]{:S(2)}) %all-to-all-start.2) | async-done | bytes 4194336 | tf_op jit(solution)/shard_map/all_to_all | solution.py:79
  326.7 2.7 copy.57
  329.4 7.1 %convolution_bitcast_fusion.2 = f32[2,256,16,128]{3,1,2,0:T(8,128)S(1)} fusion(f32[2,256,16,128,1]{3,1,0,2,4:T(8,128)S(1)} %bitcast.160, f32[1,2,256,256]{3,2,1,0:T(8,128)S(1)} %get-tuple-element.10, f32[1,2,256,256]{3,2,1,0:T(8,128)S(1)} %get-tuple-element.9), kind=kOutput, calls=%fused_computation.10 | convolution fusion | flops 6442713088 | bytes 9437184 | tf_op jit(solution)/shard_map/itnxy,oikn->otkxy/dot_general | solution.py:50
  338.1 7.4 %fusion.3 = f32[2,1,256,16,128]{4,2,3,0,1:T(8,128)S(1)} fusion(f32[1,2,256,256]{3,2,1,0:T(8,128)S(1)} %get-tuple-element.8, f32[1,2,256,256]{3,2,1,0:T(8,128)S(1)} %get-tuple-element.7, f32[1,1,256,16,128]{4,2,3,1,0:T(8,128)S(1)} %get-tuple-element.6, f32[1,1,256,16,128]{4,2,3,1,0:T(8,128)S(1)} %get-tuple-element.5), kind=kOutput, calls=%fused_computation.8 | convolution fusion | flops 6443761664 | bytes 9437184 | tf_op jit(solution)/shard_map/itnxy,oikn->otkxy/dot_general | solution.py:50
  347.9 64.3 %all_to_all.65 = f32[2,1,256,16,128]{4,3,0,1,2:T(8,128)S(1)} all-to-all(f32[2,1,256,16,128]{4,3,0,1,2:T(8,128)S(1)} %copy.64), channel_id=1, replica_groups=mesh['sta'=2,'gx'=16,'gy'=4] {'gx'}, dimensions={2} | all-to-all | bytes 8388608 | tf_op jit(solution)/shard_map/all_to_all | solution.py:87
  412.8 6.9 %convolution_bitcast_fusion.1 = f32[2,1,16,256,128]{4,3,2,0,1:T(8,128)S(1)} fusion(f32[2,16,256,128,1]{3,2,0,1,4:T(8,128)S(1)} %bitcast.159, f32[1,2,256,256]{3,2,1,0:T(8,128)S(1)} %get-tuple-element.8, f32[1,2,256,256]{3,2,1,0:T(8,128)S(1)} %get-tuple-element.7), kind=kOutput, calls=%fused_computation.9 | convolution fusion | flops 6442713088 | bytes 9437184 | tf_op jit(solution)/shard_map/itzny,oikn->otzky/dot_general | solution.py:46
  419.7 4.4 copy.66
  424.1 5.1 %all-to-all-start.4 = ((f32[2,1,16,256,128]{4,2,0,1,3:T(8,128)}), f32[2,1,16,256,128]{4,2,0,1,3:T(8,128)}, u32[]{:S(2)}, u32[]{:S(2)}) async-start(f32[2,1,16,256,128]{4,2,0,1,3:T(8,128)} %copy.66), calls=%async_computation.4 | async-start | bytes 8388608 | tf_op jit(solution)/shard_map/all_to_all | solution.py:93
  429.1 4.2 multiply_negate_fusion
  433.3 44.5 %all-to-all-done.4 = f32[2,1,16,256,128]{4,2,0,1,3:T(8,128)} async-done(((f32[2,1,16,256,128]{4,2,0,1,3:T(8,128)}), f32[2,1,16,256,128]{4,2,0,1,3:T(8,128)}, u32[]{:S(2)}, u32[]{:S(2)}) %all-to-all-start.4) | async-done | bytes 4194336 | tf_op jit(solution)/shard_map/all_to_all | solution.py:93
  477.7 6.8 %copy.94 = f32[2,1,16,4,64,128]{5,3,4,0,2,1:T(4,128)} copy(f32[2,1,16,4,64,128]{5,2,0,4,3,1:T(8,128)} %bitcast.57) | data formatting | bytes 8388608 | tf_op jit(solution)/shard_map/all_to_all | solution.py:93
  484.6 5.5 %reshape.270 = f32[2,16,64,512]{3,2,0,1:T(8,128)} reshape(f32[2,1,16,64,4,128]{5,4,3,0,2,1:T(4,128)} %bitcast.162) | data formatting | bytes 8388608 | tf_op jit(solution)/shard_map/reshape.26
  490.1 9.9 %fusion.17 = f32[1,16,64,512]{3,2,1,0:T(8,128)} fusion(f32[2,16,64,512]{3,2,0,1:T(8,128)} %reshape.270, f32[1,512,512]{2,1,0:T(8,128)S(1)} %get-tuple-element.17, f32[1,512,512]{2,1,0:T(8,128)S(1)} %get-tuple-element.18), kind=kOutput, calls=%fused_computation.32 | convolution fusion | flops 6442975232 | bytes 8388608 | tf_op jit(solution)/shard_map/itzxk,iyk->tzxy/dot_general | solution.py:91
  (28 shorter events, 9.8 us)
Async XLA Ops:
  0.0 14.8 %copy-start = (f32[128,1024]{1,0:T(8,128)S(1)}, f32[128,1024]{1,0:T(8,128)}, u32[]{:S(2)}) copy-start(f32[128,1024]{1,0:T(8,128)} %param.6) | copy-start | bytes 1572868
  7.5 7.1 %copy-start.4 = (s32[128,16]{0,1:T(8,128)S(1)}, s32[128,16]{0,1:T(8,128)}, u32[]{:S(2)}) copy-start(s32[128,16]{0,1:T(8,128)} %param.7) | copy-start | bytes 24580
  7.5 99.5 %all-to-all-start = ((bf16[2,64,64,512]{3,2,1,0:T(8,128)(2,1)}), bf16[2,64,64,512]{3,2,1,0:T(8,128)(2,1)}, u32[]{:S(2)}, u32[]{:S(2)}) async-start(bf16[2,64,64,512]{3,2,1,0:T(8,128)(2,1)} %pad_maximum_fusion), calls=%async_computation | async-start | bytes 16777216 | tf_op jit(solution)/shard_map/all_to_all | solution.py:63
  14.8 16.8 %copy-start.5 = (s32[128]{0:T(128)S(1)}, s32[128]{0:T(128)}, u32[]{:S(2)}) copy-start(s32[128]{0:T(128)} %param.8) | copy-start | bytes 1540
  164.6 53.5 %all-to-all-start.1 = ((f32[4,1,262144]{2,1,0:T(1,128)}), f32[4,1,262144]{2,1,0:T(1,128)}, u32[]{:S(2)}, u32[]{:S(2)}) async-start(f32[4,1,262144]{2,1,0:T(1,128)} %reshape.299), calls=%async_computation.1 | async-start | bytes 8388608 | tf_op jit(solution)/shard_map/all_to_all | solution.py:75
  263.2 63.5 %all-to-all-start.2 = ((f32[2,1,16,256,128]{4,2,0,1,3:T(8,128)}), f32[2,1,16,256,128]{4,2,0,1,3:T(8,128)}, u32[]{:S(2)}, u32[]{:S(2)}) async-start(f32[2,1,16,256,128]{4,2,0,1,3:T(8,128)} %copy.56), calls=%async_computation.2 | async-start | bytes 8388608 | tf_op jit(solution)/shard_map/all_to_all | solution.py:79
  329.4 7.2 %copy-start.2 = (f32[256,16,128]{2,1,0:T(8,128)S(1)}, f32[256,16,128]{2,1,0:T(8,128)}, u32[]{:S(2)}) copy-start(f32[256,16,128]{2,1,0:T(8,128)} %param.11) | copy-start | bytes 6291460
  329.4 7.2 %copy-start.3 = (f32[256,16,128]{2,1,0:T(8,128)S(1)}, f32[256,16,128]{2,1,0:T(8,128)}, u32[]{:S(2)}) copy-start(f32[256,16,128]{2,1,0:T(8,128)} %param.10) | copy-start | bytes 6291460
  424.1 53.7 %all-to-all-start.4 = ((f32[2,1,16,256,128]{4,2,0,1,3:T(8,128)}), f32[2,1,16,256,128]{4,2,0,1,3:T(8,128)}, u32[]{:S(2)}, u32[]{:S(2)}) async-start(f32[2,1,16,256,128]{4,2,0,1,3:T(8,128)} %copy.66), calls=%async_computation.4 | async-start | bytes 8388608 | tf_op jit(solution)/shard_map/all_to_all | solution.py:93
  490.1 9.9 %copy-start.1 = (f32[128,1024]{1,0:T(8,128)S(1)}, f32[128,1024]{1,0:T(8,128)}, u32[]{:S(2)}) copy-start(f32[128,1024]{1,0:T(8,128)} %param.6) | copy-start | bytes 1572868
